TPU v7x, 256 devices: a whole 4x4x8 slice. The times are simulated.
256 devices in a mesh: seq: 32 (over x, z), tensor: 8 (over y, core).
Axes of the slice: x: 4, y: 4, z: 8, core: 2. Of those that a mesh axis runs over, the one named last changes fastest.
Arguments:
- queries: bfloat16 [10240, 4096], P('seq', 'tensor'), may hold values from -8 to 8
- key_rows: bfloat16 [10240, 1024], P('seq', 'tensor'), may hold values from -8 to 8
- value_rows: bfloat16 [10240, 1024], P('seq', 'tensor'), may hold values from -6 to 6
- out_weight: bfloat16 [4096, 8192], P('tensor', 'seq'), may hold values from -0.09375 to 0.09375
- residual_in: bfloat16 [10240, 8192], P('seq'), may hold values from -0.1796875 to 0.1796875
- norm_gain: bfloat16 [8192], replicated, may hold values from 0.099609375 to 1.8984375
- prompt_lengths: int32 [18], replicated, may hold values from 1 to 5120, 10240 in all
Outputs:
- normed: bfloat16 [10240, 8192], P('seq')
- cache_keys: bfloat16 [22528, 1024], P('seq', 'tensor')
- cache_values: bfloat16 [22528, 1024], P('seq', 'tensor')
Inputs may be any that keep to these rules, and one draw needn't show every extreme that they name: `prompt_lengths`: the 18 lengths sum to 10240, and the largest is 5120.
All inputs are finite; a program needn't handle non-finite values.
Results may differ from a plain program's by a relative error of at most 0.019.
Values may be sent and summed in bfloat16 or wider, within the bound.
No kernel may reach another device: no remote copies, remote signals or barrier semaphores. Data moves between devices by JAX's collectives and lax.ppermute only.
A program may use at most 192 MiB of HBM per device.

v0:
```python
import math
import jax
import jax.numpy as jnp
from jax import lax
from jax.sharding import PartitionSpec as P

HD = 128
PAGE = 128
SLOT_DEV = 704


def position_of(stored, per_device, devices):
    half_block = per_device // 2
    device = stored // per_device
    offset = stored % per_device
    return jnp.where(
        offset < half_block,
        device * half_block + offset,
        (2 * devices - 1 - device) * half_block + offset - half_block,
    )


def stored_row(position, per_device, devices):
    half_block = per_device // 2
    block_index = position // half_block
    device = jnp.where(block_index < devices, block_index, 2 * devices - 1 - block_index)
    offset = position % half_block + jnp.where(block_index < devices, 0, half_block)
    return device * per_device + offset


def segment_of(position, lengths):
    doc_ends = jnp.cumsum(lengths, dtype=jnp.int32)
    return jnp.sum(
        (position[:, None] >= doc_ends[None, :]).astype(jnp.int32), axis=1, dtype=jnp.int32
    )


def slot_source(slot_ids, lengths, page_size):
    padded = (lengths + page_size - 1) // page_size * page_size
    page_ends = jnp.cumsum(padded, dtype=jnp.int32)
    page_starts = page_ends - padded
    doc_ends = jnp.cumsum(lengths, dtype=jnp.int32)
    doc_starts = doc_ends - lengths
    before = (slot_ids[:, None] >= page_ends[None, :]).astype(jnp.int32)
    inside = (slot_ids[:, None] >= page_starts[None, :]).astype(jnp.int32) - before
    page_start = jnp.sum(before * padded[None, :], axis=1, dtype=jnp.int32)
    doc_start = jnp.sum(before * lengths[None, :], axis=1, dtype=jnp.int32)
    length = jnp.sum(inside * lengths[None, :], axis=1, dtype=jnp.int32)
    within = slot_ids - page_start
    is_live = within < length
    return (doc_start + within, is_live)


def body(queries, key_rows, value_rows, out_weight, residual_in, norm_gain, prompt_lengths):
    seq_count = lax.axis_size("seq")
    seq_index = lax.axis_index("seq")
    per_device = queries.shape[0]
    kv_local = key_rows.shape[1] // HD
    group_size = queries.shape[1] // (kv_local * HD)
    score_scale = 1.0 / math.sqrt(HD)
    local_rows = jnp.arange(per_device, dtype=jnp.int32) + seq_index * per_device
    my_position = position_of(local_rows, per_device, seq_count)
    my_segment = segment_of(my_position, prompt_lengths)
    grouped = queries.reshape(per_device, kv_local, group_size, HD)
    kv_width = key_rows.shape[1]
    kv_piece = lax.all_gather(
        jnp.concatenate([key_rows, value_rows], axis=1), "seq", axis=0, tiled=True
    )
    key_piece = kv_piece[:, :kv_width]
    value_piece = kv_piece[:, kv_width:]
    piece_rows = key_piece.shape[0]
    key_position = position_of(jnp.arange(piece_rows, dtype=jnp.int32), per_device, seq_count)
    key_segment = segment_of(key_position, prompt_lengths)
    allowed = (key_position[None, :] <= my_position[:, None]) & (
        key_segment[None, :] == my_segment[:, None]
    )
    top_old = jnp.full((kv_local, group_size, per_device), -1e30, jnp.float32)
    scores = (
        jnp.einsum(
            "qgjd,kgd->gjqk",
            grouped,
            key_piece.reshape(piece_rows, kv_local, HD),
            preferred_element_type=jnp.float32,
        )
        * score_scale
    )
    scores = jnp.where(allowed, scores, -1e30)
    top_new = jnp.maximum(top_old, jnp.max(scores, axis=-1))
    weights = jnp.where(allowed, jnp.exp(scores - top_new[..., None]), 0.0)
    total_new = jnp.sum(weights, axis=-1)
    accum_new = jnp.einsum(
        "gjqk,kgd->gjqd",
        weights.astype(jnp.bfloat16),
        value_piece.reshape(piece_rows, kv_local, HD),
        preferred_element_type=jnp.float32,
    )
    attended = jnp.transpose(accum_new / total_new[..., None], (2, 0, 1, 3))
    attended = attended.reshape(per_device, -1).astype(jnp.bfloat16)
    partial_value = jnp.dot(
        attended,
        lax.all_gather(out_weight, "seq", axis=1, tiled=True),
        preferred_element_type=jnp.float32,
    )
    projected = lax.psum(partial_value.astype(jnp.bfloat16), "tensor").astype(jnp.float32)
    hidden = residual_in.astype(jnp.float32) + projected
    mean_square = jnp.mean(hidden * hidden, axis=-1, keepdims=True)
    normed = (hidden * lax.rsqrt(mean_square + 1e-05) * norm_gain.astype(jnp.float32)).astype(
        jnp.bfloat16
    )
    slot_ids = seq_index * SLOT_DEV + jnp.arange(SLOT_DEV, dtype=jnp.int32)
    source, is_live = slot_source(slot_ids, prompt_lengths, PAGE)
    target = stored_row(source, per_device, seq_count)
    empty_cache = jnp.zeros((SLOT_DEV, kv_local * HD), jnp.bfloat16)
    found = is_live & (target >= 0) & (target < piece_rows)
    safe_index = jnp.clip(target, 0, piece_rows - 1)
    cache_keys = jnp.where(found[:, None], jnp.take(key_piece, safe_index, axis=0), empty_cache)
    cache_values = jnp.where(found[:, None], jnp.take(value_piece, safe_index, axis=0), empty_cache)
    return (normed, cache_keys, cache_values)


def solution(mesh):
    return jax.shard_map(
        body,
        mesh=mesh,
        in_specs=(
            P("seq", "tensor"),
            P("seq", "tensor"),
            P("seq", "tensor"),
            P("tensor", "seq"),
            P("seq", None),
            P(),
            P(),
        ),
        out_specs=(P("seq", None), P("seq", "tensor"), P("seq", "tensor")),
        check_vma=False,
    )
```

profile of v0, /device:TPU:1, one launch (start us, length us, event | category | flops | bytes accessed | tf_op | source)
XLA Modules:
  0.0 310.1 jit_solution(13555092218789178911)
XLA Ops:
  7.2 0.0 copy-start
  7.2 0.0 all-gather.3.cloned.1.call-start
  7.2 1.6 pad_maximum_fusion
  8.9 0.0 all-gather.3.cloned.1.call-update
  8.9 0.0 all-gather.5.cloned.1.call-start
  9.0 0.7 all-gather.5.cloned.1.call-update
  9.7 0.0 all-reduce.2.cloned.1.call-start
  9.7 0.7 copy.17
  10.5 0.1 reduce.2
  10.6 0.7 convert_element_type.52
  11.3 0.7 fusion.65
  12.0 0.1 copy.20
  12.1 0.1 reduce.3
  12.3 0.7 fusion.55
  13.0 0.7 fusion.64
  13.6 0.8 fusion.36
  14.5 0.1 convert_reduce_fusion.1
  14.6 0.2 convert_reduce_fusion
  14.8 4.6 %compare_and_fusion = pred[320,10240]{1,0:T(8,128)(4,1)} fusion(s32[10240]{0:T(1024)S(1)} %convert_reduce_fusion, s32[10240]{0:T(1024)S(1)} %fusion.43, s32[320]{0:T(512)S(1)} %convert_reduce_fusion.1, s32[320]{0:T(512)S(1)} %add_select_fusion.5), kind=kLoop, calls=%fused_computation.10 | loop fusion | flops 9830400 | bytes 3361280 | tf_op jit(solution)/shard_map/and | solution.py:74
  19.4 78.3 %all-gather.3.cloned.1.call-done = bf16[10240,256]{1,0:T(8,128)(2,1)} async-done(((bf16[320,256]{1,0:T(8,128)(2,1)}), bf16[10240,256]{1,0:T(8,128)(2,1)}) %all-gather.3.cloned.1.call-update) | async-done | bytes 5242896 | tf_op jit(solution)/shard_map/all_gather | solution.py:66
  97.7 0.0 copy-done
  97.7 22.9 %fusion = (f32[4,320]{1,0:T(4,128)S(1)}, f32[10240,320,4]{0,1,2:T(8,128)}) fusion(pred[320,10240]{1,0:T(8,128)(4,1)} %compare_and_fusion, bf16[10240,256]{1,0:T(8,128)(2,1)} %all-gather.3.cloned.1.call-done, bf16[320,512]{1,0:T(8,128)(2,1)S(1)} %copy-done), kind=kOutput, calls=%fused_computation.4 | convolution fusion | flops 3394763520 | bytes 58659840 | tf_op jit(solution)/shard_map/qgjd,kgd->gjqk/dot_general | solution.py:79
  120.5 22.7 %fusion.1 = f32[4,320]{1,0:T(4,128)S(1)} fusion(f32[10240,320,4]{0,1,2:T(8,128)} %get-tuple-element.14, f32[4,320]{1,0:T(4,128)S(1)} %broadcast_maximum_fusion, pred[320,10240]{1,0:T(8,128)(4,1)} %compare_and_fusion), kind=kLoop, calls=%fused_computation.5 | loop fusion | flops 65534720 | bytes 55715840 | tf_op jit(solution)/shard_map/reduce_sum | solution.py:90
  143.3 23.2 %fusion.20 = bf16[320,1,4,128]{3,0,2,1:T(8,128)(2,1)S(1)} fusion(f32[10240,320,4]{0,1,2:T(8,128)} %get-tuple-element.14, f32[4,320]{1,0:T(4,128)S(1)} %broadcast_maximum_fusion, pred[320,10240]{1,0:T(8,128)(4,1)} %compare_and_fusion, f32[4,320]{1,0:T(4,128)S(1)} %fusion.1, bf16[10240,256]{1,0:T(8,128)(2,1)} %all-gather.3.cloned.1.call-done), kind=kOutput, calls=%fused_computation.20 | convolution fusion | flops 3421306880 | bytes 58664960 | tf_op jit(solution)/shard_map/gjqk,kgd->gjqd/dot_general | solution.py:91
  166.5 0.3 copy.19
  166.8 34.2 %all-gather.5.cloned.1.call-done = bf16[512,8192]{1,0:T(8,128)(2,1)} async-done(((bf16[512,256]{1,0:T(8,128)(2,1)}), bf16[512,8192]{1,0:T(8,128)(2,1)}) %all-gather.5.cloned.1.call-update) | async-done | bytes 8388624 | tf_op jit(solution)/shard_map/all_gather | solution.py:101
  200.9 8.0 %convolution_convert_fusion = bf16[320,8192]{1,0:T(8,128)(2,1)} fusion(bf16[512,8192]{1,0:T(8,128)(2,1)} %all-gather.5.cloned.1.call-done, bf16[40,8,4,128]{3,2,1,0:T(4,128)(2,1)S(1)} %bitcast.67), kind=kOutput, calls=%fused_computation.11 | convolution fusion | flops 2686976000 | bytes 13959168 | tf_op jit(solution)/shard_map/dot_general | solution.py:99
  208.9 0.0 all-reduce.2.cloned.1.call-update
  208.9 3.7 %fusion.62 = (bf16[10240,128]{1,0:T(8,128)(2,1)S(1)}, bf16[10240,128]{1,0:T(8,128)(2,1)}) fusion(bf16[10240,256]{1,0:T(8,128)(2,1)} %all-gather.3.cloned.1.call-done), kind=kLoop, calls=%fused_computation.91 | loop fusion | bytes 10485760 | tf_op jit(solution)/shard_map/slice | solution.py:70
  212.6 3.8 %gather_fusion = bf16[704,128]{1,0:T(8,128)(2,1)S(1)} fusion(bf16[10240,128]{1,0:T(8,128)(2,1)} %get-tuple-element.10, s32[1024]{0:T(1024)S(1)} %pad_clamp_fusion), kind=kCustom, calls=%fused_computation.clone | custom fusion | bytes 363264 | tf_op jit(solution)/shard_map/jit(_take)/gather | solution.py:116
  216.5 2.0 gather_fusion.1
  218.5 1.0 select_select_fusion
  219.5 71.0 %all-reduce.2.cloned.1.call-done = bf16[320,8192]{1,0:T(8,128)(2,1)} async-done(((bf16[320,8192]{1,0:T(8,128)(2,1)}), bf16[320,8192]{1,0:T(8,128)(2,1)}) %all-reduce.2.cloned.1.call-update) | async-done | bytes 5242896 | tf_op jit(solution)/shard_map/psum | solution.py:104
  290.5 0.0 copy-start.2
  290.5 0.0 copy-start.1
  290.5 6.0 %multiply_reduce_fusion = f32[320]{0:T(512)S(1)} fusion(bf16[320,8192]{1,0:T(8,128)(2,1)} %all-reduce.2.cloned.1.call-done, bf16[320,8192]{1,0:T(8,128)(2,1)} %param.13), kind=kLoop, calls=%fused_computation.13 | loop fusion | flops 13106880 | bytes 10487040 | tf_op jit(solution)/shard_map/reduce_sum | solution.py:106
  296.5 0.0 copy-done.2
  296.5 7.1 %multiply_convert_fusion = bf16[320,8192]{1,0:T(8,128)(2,1)} fusion(bf16[320,8192]{1,0:T(8,128)(2,1)S(1)} %copy-done.2, bf16[320,8192]{1,0:T(8,128)(2,1)} %param.13, f32[8192]{0:T(1024)S(1)} %convert_element_type.52, f32[320]{0:T(512)S(1)} %add_rsqrt_fusion), kind=kLoop, calls=%fused_computation.12 | loop fusion | flops 15728640 | bytes 15762688 | tf_op jit(solution)/shard_map/convert_element_type | solution.py:107
  303.6 0.0 copy-done.1
  (11 shorter events, 0.2 us)
Async XLA Ops:
  7.2 90.5 %copy-start = (bf16[320,512]{1,0:T(8,128)(2,1)S(1)}, bf16[320,512]{1,0:T(8,128)(2,1)}, u32[]{:S(2)}) copy-start(bf16[320,512]{1,0:T(8,128)(2,1)} %param.9) | copy-start | bytes 983044
  7.2 90.5 %all-gather.3.cloned.1.call-start = ((), (), s32[]{:S(2)}) async-start(), calls=%async_computation | async-start | bytes 5406720 | tf_op jit(solution)/shard_map/all_gather | solution.py:66
  8.9 192.0 %all-gather.5.cloned.1.call-start = ((), (), s32[]{:S(2)}) async-start(), calls=%async_computation.1 | async-start | bytes 8650752 | tf_op jit(solution)/shard_map/all_gather | solution.py:101
  9.7 280.8 %all-reduce.2.cloned.1.call-start = ((), (), s32[]{:S(2)}) async-start(), calls=%async_computation.2 | async-start | bytes 10485760 | tf_op jit(solution)/shard_map/psum | solution.py:104
  290.5 6.0 %copy-start.2 = (bf16[320,8192]{1,0:T(8,128)(2,1)S(1)}, bf16[320,8192]{1,0:T(8,128)(2,1)}, u32[]{:S(2)}) copy-start(bf16[320,8192]{1,0:T(8,128)(2,1)} %all-reduce.2.cloned.1.call-done) | copy-start | bytes 15728644
  290.5 13.1 %copy-start.1 = (bf16[320,512]{1,0:T(8,128)(2,1)S(1)}, bf16[320,512]{1,0:T(8,128)(2,1)}, u32[]{:S(2)}) copy-start(bf16[320,512]{1,0:T(8,128)(2,1)} %param.9) | copy-start | bytes 983044
Sparse Core Ops, SparseCore 0:
  11.2 86.4 all-gather.2
  100.1 100.7 all-gather.4
  209.0 81.3 all-reduce.1
where the time goes:
time: 310 us
  waiting for transfers between devices  184 us (59%)
  matrix products  54.1 us (17%)
  other arithmetic  47.3 us (15%)
  between operations  13.9 us (4%)
  local copies, waits for them, and re-layouts  10.7 us (3%)
    all_gather x1, waiting for transfers between devices, body(): lax.all_gather(jnp.concatenate([key_rows, value_rows], axis=1), 'seq', ax...  78.3 us
    psum x1, waiting for transfers between devices, body(): lax.psum(partial_value.astype(jnp.bfloat16), 'tensor').astype(jnp.float32)  71 us
    all_gather x1, waiting for transfers between devices, body(): lax.all_gather(out_weight, 'seq', axis=1, tiled=True)  34.2 us
    dot_general x1, matrix products, body(): jnp.einsum('gjqk,kgd->gjqd', weights.astype(jnp.bfloat16), value_piece.re...  23.2 us
    dot_general x1, matrix products, body(): jnp.einsum('qgjd,kgd->gjqk', grouped, key_piece.reshape(piece_rows, kv_lo...  22.9 us
    reduce_sum x1, other arithmetic, body(): total_new = jnp.sum(weights, axis=-1)  22.7 us
    dot_general x1, matrix products, body(): jnp.dot(attended, lax.all_gather(out_weight, 'seq', axis=1, tiled=True),...  7.96 us
    convert_element_type x1, other arithmetic, body(): (hidden * lax.rsqrt(mean_square + 1e-05) * norm_gain.astype(jnp.float32))...  7.13 us
  transfers between devices with their start and end apart: 3, of which 3 were waited for; matrix products, arithmetic and copies ran while one was open for 29% of the time, Pallas kernels for 0%

commit v1 on v0

--- a/solution.py
+++ b/solution.py
@@ -7,6 +7,10 @@
 HD = 128
 PAGE = 128
 SLOT_DEV = 704
+
+
+def serve_marks(load, comm_axis):
+    return lax.all_gather(load, axis_name=comm_axis).sum(axis=0)
 
 
 def position_of(stored, per_device, devices):
@@ -101,7 +105,7 @@
         lax.all_gather(out_weight, "seq", axis=1, tiled=True),
         preferred_element_type=jnp.float32,
     )
-    projected = lax.psum(partial_value.astype(jnp.bfloat16), "tensor").astype(jnp.float32)
+    projected = serve_marks(partial_value.astype(jnp.bfloat16), "tensor").astype(jnp.float32)
     hidden = residual_in.astype(jnp.float32) + projected
     mean_square = jnp.mean(hidden * hidden, axis=-1, keepdims=True)
     normed = (hidden * lax.rsqrt(mean_square + 1e-05) * norm_gain.astype(jnp.float32)).astype(

time: 310 us -> 442 us (1.43)
  waiting for transfers between devices: 184 us -> 302 us
  other arithmetic: 47.3 us -> 61 us
    all_gather x0 -> x1, waiting for transfers between devices: none -> 185 us  [serve_marks(): return lax.all_gather(load, axis_name=comm_axis).sum(axis=0)]
    psum x1 -> x0, waiting for transfers between devices: 71 us -> none  [body(): lax.psum(partial_value.astype(jnp.bfloat16), 'tensor').astype(jnp.float32)]
    reduce_sum x0 -> x1, other arithmetic: none -> 17.1 us  [serve_marks(): return lax.all_gather(load, axis_name=comm_axis).sum(axis=0)]
  transfers between devices with their start and end apart: 3 -> 3, of which waited for: 3 -> 3; matrix products, arithmetic and copies ran while one was open for 29% -> 19% of each run, Pallas kernels for 0% -> 0%
where the time goes in v1:
time: 442 us; the launch traced here: 441 us
  waiting for transfers between devices  302 us (68%)
  other arithmetic  61 us (14%)
  matrix products  54.1 us (12%)
  between operations  13.9 us (3%)
  local copies, waits for them, and re-layouts  10.8 us (2%)
    all_gather x1, waiting for transfers between devices, serve_marks(): return lax.all_gather(load, axis_name=comm_axis).sum(axis=0)  185 us
    all_gather x1, waiting for transfers between devices, body(): lax.all_gather(jnp.concatenate([key_rows, value_rows], axis=1), 'seq', ax...  82.1 us
    all_gather x1, waiting for transfers between devices, body(): lax.all_gather(out_weight, 'seq', axis=1, tiled=True)  34.1 us
    dot_general x1, matrix products, body(): jnp.einsum('gjqk,kgd->gjqd', weights.astype(jnp.bfloat16), value_piece.re...  23.2 us
    dot_general x1, matrix products, body(): jnp.einsum('qgjd,kgd->gjqk', grouped, key_piece.reshape(piece_rows, kv_lo...  22.9 us
    reduce_sum x1, other arithmetic, body(): total_new = jnp.sum(weights, axis=-1)  22.7 us
    reduce_sum x1, other arithmetic, serve_marks(): return lax.all_gather(load, axis_name=comm_axis).sum(axis=0)  17.1 us
  transfers between devices with their start and end apart: 3, of which 3 were waited for; matrix products, arithmetic and copies ran while one was open for 19% of the time, Pallas kernels for 0%

profile of v1, /device:TPU:1, one launch (start us, length us, event | category | flops | bytes accessed | tf_op | source)
XLA Modules:
  0.0 441.4 jit_solution(9128006849882406276)
XLA Ops:
  7.2 0.0 copy-start
  7.2 0.0 all-gather.5.cloned.1.call-start
  7.2 1.6 pad_maximum_fusion
  8.9 0.0 all-gather.5.cloned.1.call-update
  8.9 0.0 all-gather.7.cloned.1.call-start
  9.0 0.7 all-gather.7.cloned.1.call-update
  9.7 0.0 all-gather.9.cloned.1.call-start
  9.7 0.7 copy.17
  10.5 0.1 reduce.3
  10.6 0.1 convert_reduce_fusion.1
  10.8 0.2 convert_reduce_fusion
  11.0 4.6 %compare_and_fusion = pred[320,10240]{1,0:T(8,128)(4,1)} fusion(s32[10240]{0:T(1024)S(1)} %convert_reduce_fusion, s32[10240]{0:T(1024)S(1)} %fusion.43, s32[320]{0:T(512)S(1)} %convert_reduce_fusion.1, s32[320]{0:T(512)S(1)} %add_select_fusion.5), kind=kLoop, calls=%fused_computation.10 | loop fusion | flops 9830400 | bytes 3361280 | tf_op jit(solution)/shard_map/and | solution.py:78
  15.6 82.1 %all-gather.5.cloned.1.call-done = bf16[10240,256]{1,0:T(8,128)(2,1)} async-done(((bf16[320,256]{1,0:T(8,128)(2,1)}), bf16[10240,256]{1,0:T(8,128)(2,1)}) %all-gather.5.cloned.1.call-update) | async-done | bytes 5242896 | tf_op jit(solution)/shard_map/all_gather | solution.py:70
  97.7 0.0 copy-done
  97.7 22.9 %fusion = (f32[4,320]{1,0:T(4,128)S(1)}, f32[10240,320,4]{0,1,2:T(8,128)}) fusion(pred[320,10240]{1,0:T(8,128)(4,1)} %compare_and_fusion, bf16[10240,256]{1,0:T(8,128)(2,1)} %all-gather.5.cloned.1.call-done, bf16[320,512]{1,0:T(8,128)(2,1)S(1)} %copy-done), kind=kOutput, calls=%fused_computation.4 | convolution fusion | flops 3394763520 | bytes 58659840 | tf_op jit(solution)/shard_map/qgjd,kgd->gjqk/dot_general | solution.py:83
  120.5 22.7 %fusion.1 = f32[4,320]{1,0:T(4,128)S(1)} fusion(f32[10240,320,4]{0,1,2:T(8,128)} %get-tuple-element.14, f32[4,320]{1,0:T(4,128)S(1)} %broadcast_maximum_fusion, pred[320,10240]{1,0:T(8,128)(4,1)} %compare_and_fusion), kind=kLoop, calls=%fused_computation.5 | loop fusion | flops 65534720 | bytes 55715840 | tf_op jit(solution)/shard_map/reduce_sum | solution.py:94
  143.3 23.2 %fusion.20 = bf16[320,1,4,128]{3,0,2,1:T(8,128)(2,1)S(1)} fusion(f32[10240,320,4]{0,1,2:T(8,128)} %get-tuple-element.14, f32[4,320]{1,0:T(4,128)S(1)} %broadcast_maximum_fusion, pred[320,10240]{1,0:T(8,128)(4,1)} %compare_and_fusion, f32[4,320]{1,0:T(4,128)S(1)} %fusion.1, bf16[10240,256]{1,0:T(8,128)(2,1)} %all-gather.5.cloned.1.call-done), kind=kOutput, calls=%fused_computation.20 | convolution fusion | flops 3421306880 | bytes 58664960 | tf_op jit(solution)/shard_map/gjqk,kgd->gjqd/dot_general | solution.py:95
  166.5 0.3 copy.19
  166.8 0.0 copy-start.3
  166.8 0.0 copy-start.4
  166.8 34.1 %all-gather.7.cloned.1.call-done = bf16[512,8192]{1,0:T(8,128)(2,1)} async-done(((bf16[512,256]{1,0:T(8,128)(2,1)}), bf16[512,8192]{1,0:T(8,128)(2,1)}) %all-gather.7.cloned.1.call-update) | async-done | bytes 8388624 | tf_op jit(solution)/shard_map/all_gather | solution.py:105
  200.9 8.0 %convolution_convert_fusion = bf16[320,8192]{1,0:T(8,128)(2,1)} fusion(bf16[512,8192]{1,0:T(8,128)(2,1)} %all-gather.7.cloned.1.call-done, bf16[40,8,4,128]{3,2,1,0:T(4,128)(2,1)S(1)} %bitcast.69), kind=kOutput, calls=%fused_computation.11 | convolution fusion | flops 2686976000 | bytes 13959168 | tf_op jit(solution)/shard_map/dot_general | solution.py:103
  208.9 0.0 all-gather.9.cloned.1.call-update
  208.9 0.0 copy-done.3
  208.9 0.0 copy-done.4
  208.9 0.1 copy.20
  209.1 0.1 reduce.4
  209.2 0.1 fusion.36
  209.4 3.8 fusion.62
  213.2 3.8 gather_fusion
  217.1 2.0 gather_fusion.1
  219.1 1.0 select_select_fusion
  220.1 184.6 %all-gather.9.cloned.1.call-done = bf16[2560,8192]{1,0:T(8,128)(2,1)} async-done(((bf16[320,8192]{1,0:T(8,128)(2,1)}), bf16[2560,8192]{1,0:T(8,128)(2,1)}) %all-gather.9.cloned.1.call-update) | async-done | bytes 41943056 | tf_op jit(solution)/shard_map/all_gather | solution.py:13
  404.7 17.1 %reduce_sum.78 = bf16[320,8192]{1,0:T(8,128)(2,1)} reduce(bf16[8,320,8192]{2,1,0:T(8,128)(2,1)} %bitcast.68, bf16[]{:T(256)} %constant.116.clone.1), dimensions={0}, to_apply=%region_5.6 | reduce | flops 18350080 | bytes 47185920 | tf_op jit(solution)/shard_map/reduce_sum | solution.py:13
  421.8 0.0 copy-start.2
  421.8 0.0 copy-start.1
  421.8 6.0 %multiply_reduce_fusion = f32[320]{0:T(512)S(1)} fusion(bf16[320,8192]{1,0:T(8,128)(2,1)} %reduce_sum.78, bf16[320,8192]{1,0:T(8,128)(2,1)} %param.13), kind=kLoop, calls=%fused_computation.13 | loop fusion | flops 13106880 | bytes 10487040 | tf_op jit(solution)/shard_map/reduce_sum | solution.py:110
  427.8 0.0 copy-done.2
  427.8 7.1 %multiply_convert_fusion = bf16[320,8192]{1,0:T(8,128)(2,1)} fusion(bf16[320,8192]{1,0:T(8,128)(2,1)S(1)} %copy-done.2, bf16[320,8192]{1,0:T(8,128)(2,1)} %param.13, f32[8192]{0:T(1024)S(1)} %convert_element_type.54, f32[320]{0:T(512)S(1)} %add_rsqrt_fusion), kind=kLoop, calls=%fused_computation.12 | loop fusion | flops 15728640 | bytes 15762688 | tf_op jit(solution)/shard_map/convert_element_type | solution.py:111
  434.9 0.0 copy-done.1
  (15 shorter events, 0.2 us)
Async XLA Ops:
  7.2 90.5 %copy-start = (bf16[320,512]{1,0:T(8,128)(2,1)S(1)}, bf16[320,512]{1,0:T(8,128)(2,1)}, u32[]{:S(2)}) copy-start(bf16[320,512]{1,0:T(8,128)(2,1)} %param.9) | copy-start | bytes 983044
  7.2 90.5 %all-gather.5.cloned.1.call-start = ((), (), s32[]{:S(2)}) async-start(), calls=%async_computation | async-start | bytes 5406720 | tf_op jit(solution)/shard_map/all_gather | solution.py:70
  8.9 192.0 %all-gather.7.cloned.1.call-start = ((), (), s32[]{:S(2)}) async-start(), calls=%async_computation.1 | async-start | bytes 8650752 | tf_op jit(solution)/shard_map/all_gather | solution.py:105
  9.7 395.0 %all-gather.9.cloned.1.call-start = ((), (), s32[]{:S(2)}) async-start(), calls=%async_computation.2 | async-start | bytes 47185920 | tf_op jit(solution)/shard_map/all_gather | solution.py:13
  166.8 42.1 %copy-start.3 = (bf16[8192]{0:T(1024)(128)(2,1)S(1)}, bf16[8192]{0:T(1024)(128)(2,1)}, u32[]{:S(2)}) copy-start(bf16[8192]{0:T(1024)(128)(2,1)} %param.14) | copy-start | bytes 49156
  166.8 42.2 %copy-start.4 = (s32[18]{0:T(128)S(1)}, s32[18]{0:T(128)}, u32[]{:S(2)}) copy-start(s32[18]{0:T(128)} %param.15) | copy-start | bytes 220
  421.8 6.0 %copy-start.2 = (bf16[320,8192]{1,0:T(8,128)(2,1)S(1)}, bf16[320,8192]{1,0:T(8,128)(2,1)}, u32[]{:S(2)}) copy-start(bf16[320,8192]{1,0:T(8,128)(2,1)} %reduce_sum.78) | copy-start | bytes 15728644
  421.8 13.1 %copy-start.1 = (bf16[320,512]{1,0:T(8,128)(2,1)S(1)}, bf16[320,512]{1,0:T(8,128)(2,1)}, u32[]{:S(2)}) copy-start(bf16[320,512]{1,0:T(8,128)(2,1)} %param.9) | copy-start | bytes 983044
Sparse Core Ops, SparseCore 0:
  11.2 86.4 all-gather.4
  100.1 100.7 all-gather.6
  209.0 195.5 all-gather.8
